TPU v7x, 32 devices: a whole 2x2x4 slice. The times are simulated.
32 devices in a mesh: rep: 4 (over z), sy: 2 (over y), sx: 4 (over x, core).
Axes of the slice: x: 2, y: 2, z: 4, core: 2. Of those that a mesh axis runs over, the one named last changes fastest.
Arguments:
- features: bfloat16 [4, 32, 64, 256], P('rep', 'sy', 'sx'), may hold values from -1.5 to 1.5
- cotangent: bfloat16 [4, 32, 64, 256], P('rep', 'sy', 'sx'), may hold values from -15 to 15
- gain_conv: float32 [256], replicated, may hold values from 0.25 to 1.75
- expand_weight: bfloat16 [256, 1024], replicated, may hold values from -0.375 to 0.375
- dw_kernel: float32 [1024, 9], replicated, may hold values from -2 to 2
- project_weight: bfloat16 [1024, 256], replicated, may hold values from -0.1875 to 0.1875
- gain_block: float32 [256], replicated, may hold values from 0.25 to 1.75
- block_inward: bfloat16 [256, 768], replicated, may hold values from -0.375 to 0.375
- block_outward: bfloat16 [256, 256], replicated, may hold values from -0.375 to 0.375
- gain_grid: float32 [256], replicated, may hold values from 0.25 to 1.75
- grid_inward: bfloat16 [256, 768], replicated, may hold values from -0.375 to 0.375
- grid_outward: bfloat16 [256, 256], replicated, may hold values from -0.375 to 0.375
Outputs:
- output_tokens: bfloat16 [4, 32, 64, 256], P('rep', 'sy', 'sx')
- token_grads: bfloat16 [4, 32, 64, 256], P('rep', 'sy', 'sx')
- grad_conv_gain: float32 [256], P('rep')
- grad_expand: float32 [256, 1024], P('rep')
- grad_kernel: float32 [1024, 9], P('rep')
- grad_project: float32 [1024, 256], P('rep')
- grad_block_gain: float32 [256], P('rep')
- grad_block_inward: float32 [256, 768], P('rep')
- grad_block_outward: float32 [256, 256], P('rep')
- grad_grid_gain: float32 [256], P('rep')
- grad_grid_inward: float32 [256, 768], P('rep')
- grad_grid_outward: float32 [256, 256], P('rep')
All inputs are finite; a program needn't handle non-finite values.
Results may differ from a plain program's by a relative error of at most 0.018.
Values may be sent and summed in bfloat16 or wider, within the bound.
No kernel may reach another device: no remote copies, remote signals or barrier semaphores. Data moves between devices by JAX's collectives and lax.ppermute only.
A program may use at most 64 MiB of HBM per device.

v0:
```python
import jax
import jax.numpy as jnp
from jax import lax
from jax.sharding import PartitionSpec as P

HEADS = 8
WIN = 8
EPSILON = 1e-05


def as_sent(value):

    def short(part):
        return part.astype(jnp.bfloat16) if part.dtype == jnp.float32 else part

    return jax.tree.map(short, value)


def extended_2(cells, sides, width):
    for axis, dim in sides:
        count = lax.axis_size(axis)
        ends = count - 1
        head = lax.slice_in_dim(cells, 0, width, axis=dim)
        tail = lax.slice_in_dim(cells, cells.shape[dim] - width, cells.shape[dim], axis=dim)
        cells = jnp.concatenate(
            [
                lax.ppermute(tail, axis, [(i, (i + 1) % count) for i in range(ends)]),
                cells,
                lax.ppermute(head, axis, [((i + 1) % count, i) for i in range(ends)]),
            ],
            axis=dim,
        )
    return cells


def widen(values):
    return lax.optimization_barrier(values).astype(jnp.float32)


def layer_norm(values, gain):
    row_mean = jnp.mean(values, axis=-1, keepdims=True)
    centred = values - row_mean
    variance = jnp.mean(centred * centred, axis=-1, keepdims=True)
    return centred * lax.rsqrt(variance + EPSILON) * gain


def project_rows(values, weight):
    leading = values.shape[:-1]
    flattened = values.reshape(-1, values.shape[-1])
    product = jnp.dot(flattened, weight, preferred_element_type=jnp.float32)
    return product.reshape(leading + (weight.shape[1],))


def outer_sum(left_side, right_side):
    left_flat = left_side.reshape(-1, left_side.shape[-1])
    right_flat = right_side.reshape(-1, right_side.shape[-1]).astype(jnp.bfloat16)
    return lax.dot_general(
        left_flat, right_flat, (((0,), (0,)), ((), ())), preferred_element_type=jnp.float32
    )


def to_windows(image, side):
    height, breadth, channels = image.shape
    blocks = image.reshape(height // side, side, breadth // side, side, channels)
    return blocks.transpose(0, 2, 1, 3, 4).reshape(-1, side * side, channels)


def from_windows(windows, height, breadth, side):
    channels = windows.shape[-1]
    blocks = windows.reshape(height // side, breadth // side, side, side, channels)
    return blocks.transpose(0, 2, 1, 3, 4).reshape(height, breadth, channels)


def to_grid(image, side):
    height, breadth, channels = image.shape
    blocks = image.reshape(side, height // side, side, breadth // side, channels)
    return blocks.transpose(1, 3, 0, 2, 4).reshape(-1, side * side, channels)


def from_grid(windows, height, breadth, side):
    channels = windows.shape[-1]
    blocks = windows.reshape(height // side, breadth // side, side, side, channels)
    return blocks.transpose(2, 0, 3, 1, 4).reshape(height, breadth, channels)


def window_attention(windows, weight, tap_in, heads):
    count, members, channels = windows.shape
    head_width = channels // heads
    qkv_rows = (project_rows(windows, weight) + tap_in).astype(jnp.bfloat16)
    queries = qkv_rows[..., :channels].reshape(count, members, heads, head_width)
    key_rows = qkv_rows[..., channels : 2 * channels].reshape(count, members, heads, head_width)
    value_rows = qkv_rows[..., 2 * channels :].reshape(count, members, heads, head_width)
    scores = jnp.einsum(
        "wqhd,wkhd->whqk", queries, key_rows, preferred_element_type=jnp.float32
    ) * head_width ** (-0.5)
    softmax_out = jax.nn.softmax(scores, axis=-1).astype(jnp.bfloat16)
    attended = jnp.einsum(
        "whqk,wkhd->wqhd", softmax_out, value_rows, preferred_element_type=jnp.float32
    )
    return attended.astype(jnp.bfloat16).reshape(count, members, channels)


def depthwise(extended, kernel):
    height = extended.shape[0] - 2
    breadth = extended.shape[1] - 2
    widened = widen(extended)
    summed = jnp.zeros((height, breadth, extended.shape[2]), jnp.float32)
    for tap_index in range(9):
        row_step, col_step = divmod(tap_index, 3)
        summed = (
            summed
            + widened[row_step : row_step + height, col_step : col_step + breadth]
            * kernel[:, tap_index]
        )
    return summed


def depthwise_back(grad_ext, kernel):
    height = grad_ext.shape[0] - 2
    breadth = grad_ext.shape[1] - 2
    summed = jnp.zeros((height, breadth, grad_ext.shape[2]), jnp.float32)
    for tap_index in range(9):
        row_step, col_step = divmod(tap_index, 3)
        summed = (
            summed
            + grad_ext[2 - row_step : 2 - row_step + height, 2 - col_step : 2 - col_step + breadth]
            * kernel[:, tap_index]
        )
    return summed


def swap_blocks(blocks):
    sy_count, sx_count, row_part, col_part, channels = blocks.shape
    flattened = blocks.reshape(sy_count * sx_count, row_part, col_part, channels)
    moved = lax.all_to_all(
        as_sent(flattened), ("sy", "sx"), split_axis=0, concat_axis=0, tiled=True
    ).astype(flattened.dtype)
    return moved.reshape(blocks.shape)


def to_exchanged(image):
    height, breadth, channels = image.shape
    sy_count = lax.axis_size("sy")
    sx_count = lax.axis_size("sx")
    blocks = image.reshape(height // sy_count, sy_count, breadth // sx_count, sx_count, channels)
    moved = swap_blocks(blocks.transpose(1, 3, 0, 2, 4))
    return moved.transpose(0, 2, 1, 3, 4).reshape(height, breadth, channels)


def to_home(image):
    height, breadth, channels = image.shape
    sy_count = lax.axis_size("sy")
    sx_count = lax.axis_size("sx")
    blocks = image.reshape(sy_count, height // sy_count, sx_count, breadth // sx_count, channels)
    moved = swap_blocks(blocks.transpose(0, 2, 1, 3, 4))
    return moved.transpose(2, 0, 3, 1, 4).reshape(height, breadth, channels)


def body(
    features,
    cotangent,
    gain_conv,
    expand_weight,
    dw_kernel,
    project_weight,
    gain_block,
    block_inward,
    block_outward,
    gain_grid,
    grid_inward,
    grid_outward,
):
    image = features[0]
    height, breadth, channels = image.shape
    expand_units = expand_weight.shape[1]
    window_count = height * breadth // (WIN * WIN)
    zero_width = jnp.zeros((height, breadth, channels), jnp.float32)
    zero_expand = jnp.zeros((height, breadth, expand_units), jnp.float32)
    zero_qkv = jnp.zeros((window_count, WIN * WIN, 3 * channels), jnp.float32)
    widened = image.astype(jnp.float32)

    def conv_front(wide_in, gain_in):
        return layer_norm(wide_in, gain_in).astype(jnp.bfloat16)

    normed, front_back = jax.vjp(conv_front, widened, gain_conv)

    def expand_fn(normed_in, tap_in):
        return jax.nn.gelu(project_rows(normed_in, expand_weight) + tap_in).astype(jnp.bfloat16)

    inner, expand_back = jax.vjp(expand_fn, normed, zero_expand)
    inner_ext = extended_2(inner, (("sy", 0), ("sx", 1)), 1)

    def conv_only(kernel_in):
        return depthwise(inner_ext, kernel_in)

    conv_out, kernel_back = jax.vjp(conv_only, dw_kernel)

    def conv_tail(conv_in, wide_in, tap_in):
        activated_in = jax.nn.gelu(conv_in).astype(jnp.bfloat16)
        return (wide_in + project_rows(activated_in, project_weight) + tap_in, activated_in)

    stream_one, tail_back, activated = jax.vjp(
        conv_tail, conv_out, widened, zero_width, has_aux=True
    )

    def block_layer(stream_in, gain_in, tap_in, tap_out):
        normed_two = layer_norm(stream_in, gain_in).astype(jnp.bfloat16)
        windows = to_windows(normed_two, WIN)
        attended = window_attention(windows, block_inward, tap_in, HEADS)
        attended_home = from_windows(attended, height, breadth, WIN)
        return (
            stream_in + project_rows(attended_home, block_outward) + tap_out,
            (windows, attended_home),
        )

    stream_two, block_back, block_saved = jax.vjp(
        block_layer, stream_one, gain_block, zero_qkv, zero_width, has_aux=True
    )

    def grid_front(stream_in, gain_in):
        return layer_norm(stream_in, gain_in).astype(jnp.bfloat16)

    normed_three, grid_front_back = jax.vjp(grid_front, stream_two, gain_grid)
    grid_windows = to_grid(to_exchanged(normed_three), WIN)

    def grid_core(windows_in, tap_in):
        return window_attention(windows_in, grid_inward, tap_in, HEADS)

    grid_attended, grid_core_back = jax.vjp(grid_core, grid_windows, zero_qkv)
    grid_home = to_home(from_grid(grid_attended, height, breadth, WIN))

    def grid_tail(stream_in, attended_in, tap_in):
        return (stream_in + project_rows(attended_in, grid_outward) + tap_in).astype(jnp.bfloat16)

    output_tile, grid_tail_back = jax.vjp(grid_tail, stream_two, grid_home, zero_width)
    d_stream_two, d_grid_home, tap_grid_out = grid_tail_back(cotangent[0])
    d_grid_attended = to_grid(to_exchanged(d_grid_home), WIN)
    d_grid_windows, tap_grid_in = grid_core_back(d_grid_attended)
    d_normed_three = to_home(from_grid(d_grid_windows, height, breadth, WIN))
    d_stream_extra, d_gain_grid = grid_front_back(d_normed_three)
    d_stream_two = d_stream_two + d_stream_extra
    d_stream_one, d_gain_block, tap_block_in, tap_block_out = block_back(d_stream_two)
    d_conv, d_wide_tail, tap_project = tail_back(d_stream_one)
    d_conv_ext = extended_2(d_conv, (("sy", 0), ("sx", 1)), 1)
    d_kernel = kernel_back(d_conv)[0]
    d_inner = depthwise_back(d_conv_ext, dw_kernel).astype(jnp.bfloat16)
    d_normed, tap_expand = expand_back(d_inner)
    d_wide_front, d_gain_conv = front_back(d_normed)
    token_grad = (d_wide_tail + d_wide_front).astype(jnp.bfloat16)
    local_grads = (
        d_gain_conv,
        outer_sum(normed, tap_expand),
        d_kernel,
        outer_sum(activated, tap_project),
        d_gain_block,
        outer_sum(block_saved[0], tap_block_in),
        outer_sum(block_saved[1], tap_block_out),
        d_gain_grid,
        outer_sum(grid_windows, tap_grid_in),
        outer_sum(grid_home, tap_grid_out),
    )
    whole_sums = lax.psum(
        (
            local_grads[0],
            local_grads[1],
            local_grads[2],
            local_grads[3],
            local_grads[4],
            local_grads[5],
            local_grads[6],
            local_grads[7],
            local_grads[8],
            local_grads[9],
        ),
        ("sy", "sx"),
    )
    summed = (
        lax.psum_scatter(whole_sums[0], "rep", scatter_dimension=0, tiled=True),
        lax.psum_scatter(whole_sums[1], "rep", scatter_dimension=0, tiled=True),
        lax.psum_scatter(whole_sums[2], "rep", scatter_dimension=0, tiled=True),
        lax.psum_scatter(whole_sums[3], "rep", scatter_dimension=0, tiled=True),
        lax.psum_scatter(whole_sums[4], "rep", scatter_dimension=0, tiled=True),
        lax.psum_scatter(whole_sums[5], "rep", scatter_dimension=0, tiled=True),
        lax.psum_scatter(whole_sums[6], "rep", scatter_dimension=0, tiled=True),
        lax.psum_scatter(whole_sums[7], "rep", scatter_dimension=0, tiled=True),
        lax.psum_scatter(whole_sums[8], "rep", scatter_dimension=0, tiled=True),
        lax.psum_scatter(whole_sums[9], "rep", scatter_dimension=0, tiled=True),
    )
    return (
        output_tile[None],
        token_grad[None],
        summed[0],
        summed[1],
        summed[2],
        summed[3],
        summed[4],
        summed[5],
        summed[6],
        summed[7],
        summed[8],
        summed[9],
    )


def solution(mesh):
    return jax.shard_map(
        body,
        mesh=mesh,
        in_specs=(
            P("rep", "sy", "sx", None),
            P("rep", "sy", "sx", None),
            P(),
            P(),
            P(),
            P(),
            P(),
            P(),
            P(),
            P(),
            P(),
            P(),
        ),
        out_specs=(
            P("rep", "sy", "sx", None),
            P("rep", "sy", "sx", None),
            P("rep"),
            P("rep", None),
            P("rep", None),
            P("rep", None),
            P("rep"),
            P("rep", None),
            P("rep", None),
            P("rep"),
            P("rep", None),
            P("rep", None),
        ),
        check_vma=False,
    )
```

profile of v0, /device:TPU:0, one launch (start us, length us, event | category | flops | bytes accessed | tf_op | source)
XLA Modules:
  0.0 337.4 jit_solution(8117348626632107201)
XLA Ops:
  9.5 2.4 multiply_convert_fusion.1
  11.8 1.4 collective-permute-start.1
  13.3 4.9 %collective-permute-start = (bf16[1,16,1024]{2,1,0:T(8,128)(2,1)S(1)}, bf16[1,16,1024]{2,1,0:T(8,128)(2,1)S(1)}, u32[]{:S(2)}, u32[]{:S(2)}) collective-permute-start(bf16[1,16,1024]{2,1,0:T(8,128)(2,1)S(1)} %get-tuple-element.51), channel_id=1, source_target_pairs={{0,4},{1,5},{2,6},{3,7},{8,12},{9,13},{10,14},{11,15},{16,20},{17,... | collective-permute-start | bytes 98312 | tf_op jit(solution)/shard_map/ppermute | solution.py:27
  19.2 4.0 %all-to-all-start.2 = ((bf16[8,8,4,256]{3,1,2,0:T(8,128)(2,1)}), bf16[8,8,4,256]{3,1,2,0:T(8,128)(2,1)}, u32[]{:S(2)}, u32[]{:S(2)}) async-start(bf16[8,8,4,256]{3,1,2,0:T(8,128)(2,1)} %bitcast.44), calls=%async_computation.2 | async-start | bytes 262144 | tf_op jit(solution)/shard_map/all_to_all | solution.py:135
  23.3 1.3 collective-permute-start.3
  24.6 3.0 collective-permute-start.2
  33.3 3.2 fusion.105
  36.5 1.5 fusion.6
  39.3 1.2 fusion.106
  42.3 6.7 %all-to-all-start = ((bf16[8,8,4,256]{3,1,2,0:T(8,128)(2,1)}), bf16[8,8,4,256]{3,1,2,0:T(8,128)(2,1)}, u32[]{:S(2)}, u32[]{:S(2)}) async-start(bf16[8,8,4,256]{3,1,2,0:T(8,128)(2,1)} %bitcast.24), calls=%async_computation | async-start | bytes 262144 | tf_op jit(solution)/shard_map/all_to_all | solution.py:135
  50.8 1.2 reshape_reshape.26
  53.1 1.6 all-to-all-done
  55.8 1.3 convolution_convert_fusion.3
  57.8 1.7 copy.143
  59.5 1.7 copy.144
  62.1 2.6 fusion.107
  64.7 1.8 fusion.15
  69.8 1.8 copy.160
  71.6 1.7 copy.158
  73.3 1.7 copy.156
  77.4 7.9 %all_to_all.20 = bf16[8,8,4,256]{3,1,2,0:T(8,128)(2,1)S(1)} all-to-all(bf16[8,8,4,256]{3,1,2,0:T(8,128)(2,1)S(1)} %bitcast.291), channel_id=1, replica_groups=mesh['rep'=4,'sy'=2,'sx'=4] {'sy','sx'}, dimensions={0} | all-to-all | bytes 262144 | tf_op jit(solution)/shard_map/all_to_all | solution.py:135
  88.2 1.5 multiply_reduce_fusion.9
  89.7 1.6 fusion.96
  92.5 2.2 fusion.7
  94.7 2.1 copy.147
  96.8 2.1 reshape.413
  98.9 1.7 copy.148
  100.6 1.6 reshape_reshape.24
  103.1 7.9 %all_to_all.21 = bf16[8,8,4,256]{3,1,2,0:T(8,128)(2,1)S(1)} all-to-all(bf16[8,8,4,256]{3,1,2,0:T(8,128)(2,1)S(1)} %bitcast.293), channel_id=1, replica_groups=mesh['rep'=4,'sy'=2,'sx'=4] {'sy','sx'}, dimensions={0} | all-to-all | bytes 262144 | tf_op jit(solution)/shard_map/all_to_all | solution.py:135
  111.8 1.6 reshape_reshape.29
  113.4 1.9 fusion.112
  115.3 1.3 multiply_divide_fusion
  116.7 1.2 fusion.111
  117.9 1.2 fusion.114
  119.8 1.2 reshape.428
  122.1 1.9 fusion.20
  124.0 1.9 convolution_convert_fusion.5
  127.0 2.5 convolution_convert_fusion.6
  129.5 1.7 copy.170
  131.2 2.4 convolution_convert_fusion.7
  133.7 1.7 copy.167
  136.8 2.1 fusion.109
  139.9 1.1 add_add_fusion.4
  142.3 1.6 convolution_bitcast_fusion
  144.1 3.7 %multiply_reduce_fusion.8 = (f32[1024]{0:T(1024)S(1)}, f32[1024]{0:T(1024)S(1)}, f32[1024]{0:T(1024)S(1)}, f32[1024]{0:T(1024)S(1)}, f32[1024]{0:T(1024)S(1)}, /...) fusion(f32[18,18,1024]{2,1,0:T(8,128)S(1)} %convert_element_typ, ...), kind=kLoop, calls=%fused_computation.104 | loop fusion | flops 14408704 | bytes 11083776 | tf_op jit(solution)/shard_map/transpose(jvp())/reduce_sum | solution.py:112
  147.8 1.3 collective-permute-start.5
  149.1 4.5 %collective-permute-start.4 = (f32[1,16,1024]{2,1,0:T(8,128)S(1)}, f32[1,16,1024]{2,1,0:T(8,128)S(1)}, u32[]{:S(2)}, u32[]{:S(2)}) collective-permute-start(f32[1,16,1024]{2,1,0:T(8,128)S(1)} %get-tuple-element.47), channel_id=1, source_target_pairs={{0,4},{1,5},{2,6},{3,7},{8,12},{9,13},{10,14},{11,15},{16,20},{17,... | collective-permute-start | bytes 196616 | tf_op jit(solution)/shard_map/ppermute | solution.py:27
  153.9 1.6 collective-permute-done.4
  155.6 1.3 collective-permute-start.6
  156.9 3.0 collective-permute-start.7
  161.4 1.9 fusion.22
  163.3 1.3 fusion.108
  168.5 15.5 %reduce-scatter.14.cloned.1.call-done = f32[64,768]{1,0:T(8,128)} async-done(((f32[256,768]{1,0:T(8,128)}), f32[64,768]{1,0:T(8,128)}) %reduce-scatter.14.cloned.1.call-update) | async-done | bytes 196624 | tf_op jit(solution)/shard_map/reduce_scatter | solution.py:283
  184.1 28.8 %reduce-scatter.12.cloned.1.call-done = f32[256,256]{1,0:T(8,128)} async-done(((f32[1024,256]{1,0:T(8,128)}), f32[256,256]{1,0:T(8,128)}) %reduce-scatter.12.cloned.1.call-update) | async-done | bytes 262160 | tf_op jit(solution)/shard_map/reduce_scatter | solution.py:281
  212.8 28.1 %reduce-scatter.8.cloned.1.call-done = f32[64,1024]{1,0:T(8,128)} async-done(((f32[256,1024]{1,0:T(8,128)}), f32[64,1024]{1,0:T(8,128)}) %reduce-scatter.8.cloned.1.call-update) | async-done | bytes 262160 | tf_op jit(solution)/shard_map/reduce_scatter | solution.py:279
  241.3 9.4 %all-reduce.20 = (f32[256]{0:T(256)S(1)}, f32[256]{0:T(256)S(1)}, f32[256]{0:T(256)S(1)}) all-reduce(f32[256]{0:T(256)S(1)} %get-tuple-element.25, f32[256]{0:T(256)S(1)} %copy-done.52, f32[256]{0:T(256)S(1)} %copy-done.51), channel_id=2, replica_groups=mesh['rep'=4,'sy'=2,'sx'=4] {'rep'}, use_global_device_ids=true, to_apply=%region_20.0.clone | all-reduce | flops 768 | bytes 6144
  250.9 10.5 %reduce-scatter.10.cloned.1.call-done = f32[256,9]{0,1:T(8,128)} async-done(((f32[1024,9]{0,1:T(8,128)}), f32[256,9]{0,1:T(8,128)}) %reduce-scatter.10.cloned.1.call-update) | async-done | bytes 9232 | tf_op jit(solution)/shard_map/reduce_scatter | solution.py:280
  261.5 23.7 %all-reduce.18 = (f32[64]{0:T(128)}, f32[256,9]{0,1:T(8,128)}, f32[64]{0:T(128)}, f32[64]{0:T(128)}) all-reduce(f32[64]{0:T(128)S(1)} %dynamic-slice.1, f32[256,9]{0,1:T(8,128)} %reduce-scatter.10.cloned.1.call-done, f32[64]{0:T(128)S(1)} %dynamic-slice.3, f32[64]{0:T(128)S(1)} %dynamic-slice.5), channel_id=1, replica_groups=mesh['rep'=4,'sy'=2,'sx'=4] {'sy','sx'}, use_global_device_ids=true, to_apply=%region_19.0 | all-reduce | flops 2496 | bytes 19968 | tf_op jit(solution)/shard_map/psum | solution.py:262
  286.0 35.9 %all-reduce.23.cloned.1.call-done = (f32[64,1024]{1,0:T(8,128)}, f32[256,256]{1,0:T(8,128)}, f32[64,768]{1,0:T(8,128)}, f32[64,256]{1,0:T(8,128)}, f32[64,768]{1,0:T(8,128)}, /*index=5*/f32[64,256]{1,0:T(8,128)}) async-done(((f32[64,1024]{1,0:T(8,128)}, f32[256,256]{1,0:T(8,128)}, f32[64,768]{1,0:T(8,128)}, f32[64,256]{1,0:T(8,128)}, f32[64,768]{1,0:T(8,128)}, /*index=5*/f32[64,256]{1,0:T(8,128)}), ...) | async-done | bytes 1048592 | tf_op jit(solution)/shard_map/psum | solution.py:262
  321.9 1.7 copy.199
  323.6 1.7 copy.200
  325.2 1.6 copy.201
  326.9 1.5 copy.202
  328.3 1.6 copy.203
  (231 shorter events, 42.0 us)
Async XLA Ops:
  7.2 2.3 copy-start
  8.3 9.9 %copy-start.8 = (bf16[1,16,16,256]{3,2,1,0:T(8,128)(2,1)S(1)}, bf16[1,16,16,256]{3,2,1,0:T(8,128)(2,1)}, u32[]{:S(2)}) copy-start(bf16[1,16,16,256]{3,2,1,0:T(8,128)(2,1)} %param.13) | copy-start | bytes 393220
  8.3 9.9 %copy-start.20 = (bf16[256,256]{1,0:T(8,128)(2,1)S(1)}, bf16[256,256]{1,0:T(8,128)(2,1)}, u32[]{:S(2)}) copy-start(bf16[256,256]{1,0:T(8,128)(2,1)} %param.23) | copy-start | bytes 393220
  11.8 15.8 %copy-start.45 = (f32[1024,9]{0,1:T(8,128)S(1)}, f32[1024,9]{0,1:T(8,128)}, u32[]{:S(2)}) copy-start(f32[1024,9]{0,1:T(8,128)} %param.16) | copy-start | bytes 110596
  11.8 11.3 %collective-permute-start.1 = (bf16[1,16,1024]{2,1,0:T(8,128)(2,1)S(1)}, bf16[1,16,1024]{2,1,0:T(8,128)(2,1)S(1)}, u32[]{:S(2)}, u32[]{:S(2)}) collective-permute-start(bf16[1,16,1024]{2,1,0:T(8,128)(2,1)S(1)} %get-tuple-element.52), channel_id=1, source_target_pairs={{4,0},{5,1},{6,2},{7,3},{12,8},{13,9},{14,10},{15,11},{20,16},{21,... | collective-permute-start | bytes 98312 | tf_op jit(solution)/shard_map/ppermute | solution.py:29
  13.3 9.9 %collective-permute-start = (bf16[1,16,1024]{2,1,0:T(8,128)(2,1)S(1)}, bf16[1,16,1024]{2,1,0:T(8,128)(2,1)S(1)}, u32[]{:S(2)}, u32[]{:S(2)}) collective-permute-start(bf16[1,16,1024]{2,1,0:T(8,128)(2,1)S(1)} %get-tuple-element.51), channel_id=1, source_target_pairs={{0,4},{1,5},{2,6},{3,7},{8,12},{9,13},{10,14},{11,15},{16,20},{17,... | collective-permute-start | bytes 98312 | tf_op jit(solution)/shard_map/ppermute | solution.py:27
  19.2 23.1 %all-to-all-start.2 = ((bf16[8,8,4,256]{3,1,2,0:T(8,128)(2,1)}), bf16[8,8,4,256]{3,1,2,0:T(8,128)(2,1)}, u32[]{:S(2)}, u32[]{:S(2)}) async-start(bf16[8,8,4,256]{3,1,2,0:T(8,128)(2,1)} %bitcast.44), calls=%async_computation.2 | async-start | bytes 262144 | tf_op jit(solution)/shard_map/all_to_all | solution.py:135
  23.3 4.5 %collective-permute-start.3 = (bf16[18,1,1024]{2,1,0:T(2,128)(2,1)S(1)}, bf16[18,1,1024]{2,1,0:T(2,128)(2,1)S(1)}, u32[]{:S(2)}, u32[]{:S(2)}) collective-permute-start(bf16[18,1,1024]{2,1,0:T(2,128)(2,1)S(1)} %get-tuple-element.50), channel_id=1, source_target_pairs={{1,0},{2,1},{3,2},{5,4},{6,5},{7,6},{9,8},{10,9},{11,10},{13,12},{... | collective-permute-start | bytes 110600 | tf_op jit(solution)/shard_map/ppermute | solution.py:29
  24.6 3.9 %collective-permute-start.2 = (bf16[18,1,1024]{2,1,0:T(2,128)(2,1)S(1)}, bf16[18,1,1024]{2,1,0:T(2,128)(2,1)S(1)}, u32[]{:S(2)}, u32[]{:S(2)}) collective-permute-start(bf16[18,1,1024]{2,1,0:T(2,128)(2,1)S(1)} %get-tuple-element.49), channel_id=1, source_target_pairs={{0,1},{1,2},{2,3},{4,5},{5,6},{6,7},{8,9},{9,10},{10,11},{12,13},{... | collective-permute-start | bytes 110600 | tf_op jit(solution)/shard_map/ppermute | solution.py:27
  27.7 1.5 copy-start.30
  27.7 1.5 copy-start.32
  27.7 1.5 copy-start.34
  27.7 1.5 copy-start.36
  27.8 1.5 copy-start.38
  27.8 1.5 copy-start.40
  27.8 1.5 copy-start.42
  30.4 1.3 copy-start.5
  31.6 4.8 %copy-start.7 = (bf16[2,8,2,8,256]{4,3,1,2,0:T(8,128)(2,1)}, bf16[2,8,2,8,256]{4,3,1,2,0:T(8,128)(2,1)S(1)}, u32[]{:S(2)}) copy-start(bf16[2,8,2,8,256]{4,3,1,2,0:T(8,128)(2,1)S(1)} %copy.133) | copy-start | bytes 393220
  32.2 4.2 %copy-start.18 = (bf16[4,64,256]{1,2,0:T(8,128)(2,1)}, bf16[4,64,256]{1,2,0:T(8,128)(2,1)S(1)}, u32[]{:S(2)}) copy-start(bf16[4,64,256]{1,2,0:T(8,128)(2,1)S(1)} %copy.134) | copy-start | bytes 393220
  33.3 3.2 copy-start.26
  42.3 12.4 %all-to-all-start = ((bf16[8,8,4,256]{3,1,2,0:T(8,128)(2,1)}), bf16[8,8,4,256]{3,1,2,0:T(8,128)(2,1)}, u32[]{:S(2)}, u32[]{:S(2)}) async-start(bf16[8,8,4,256]{3,1,2,0:T(8,128)(2,1)} %bitcast.24), calls=%async_computation | async-start | bytes 262144 | tf_op jit(solution)/shard_map/all_to_all | solution.py:135
  49.1 119.4 %reduce-scatter.16.cloned.1.call-start = ((), (), s32[]{:S(2)}) async-start(), calls=%async_computation.15 | async-start | bytes 327680 | tf_op jit(solution)/shard_map/reduce_scatter | solution.py:284
  57.0 7.6 %copy-start.17 = (bf16[4,64,8,32]{1,3,2,0:T(8,128)(2,1)S(1)}, bf16[4,64,8,32]{1,3,2,0:T(8,128)(2,1)}, u32[]{:S(2)}) copy-start(bf16[4,64,8,32]{1,3,2,0:T(8,128)(2,1)} %copy.154) | copy-start | bytes 393220
  64.7 4.0 %copy-start.49 = (f32[4,8,64]{2,1,0:T(8,128)}, f32[4,8,64]{2,1,0:T(8,128)S(1)}, u32[]{:S(2)}) copy-start(f32[4,8,64]{2,1,0:T(8,128)S(1)} %get-tuple-element.80) | copy-start | bytes 24580
  64.7 1.9 copy-start.16
  64.7 1.9 copy-start.29
  69.8 7.0 %copy-start.4 = (bf16[256,768]{1,0:T(8,128)(2,1)S(1)}, bf16[256,768]{1,0:T(8,128)(2,1)}, u32[]{:S(2)}) copy-start(bf16[256,768]{1,0:T(8,128)(2,1)} %param.22) | copy-start | bytes 1179652
  77.1 12.6 %copy-start.9 = (bf16[1,16,16,256]{3,2,1,0:T(8,128)(2,1)S(1)}, bf16[1,16,16,256]{3,2,1,0:T(8,128)(2,1)}, u32[]{:S(2)}) copy-start(bf16[1,16,16,256]{3,2,1,0:T(8,128)(2,1)} %param.13) | copy-start | bytes 393220
  87.2 4.0 %copy-start.12 = (bf16[2,8,2,8,256]{4,3,2,1,0:T(8,128)(2,1)S(1)}, bf16[2,8,2,8,256]{4,3,2,1,0:T(8,128)(2,1)}, u32[]{:S(2)}) copy-start(bf16[2,8,2,8,256]{4,3,2,1,0:T(8,128)(2,1)} %copy-done.11) | copy-start | bytes 393220
  92.2 76.3 %reduce-scatter.20.cloned.1.call-start = ((), (), s32[]{:S(2)}) async-start(), calls=%async_computation.17 | async-start | bytes 327680 | tf_op jit(solution)/shard_map/reduce_scatter | solution.py:287
  94.7 22.0 %copy-start.3 = (bf16[4,64,768]{2,1,0:T(8,128)(2,1)S(1)}, bf16[4,64,768]{2,1,0:T(8,128)(2,1)}, u32[]{:S(2)}) copy-start(bf16[4,64,768]{2,1,0:T(8,128)(2,1)} %copy-done.2) | copy-start | bytes 1179652
  115.3 53.2 %reduce-scatter.18.cloned.1.call-start = ((), (), s32[]{:S(2)}) async-start(), calls=%async_computation.16 | async-start | bytes 983040 | tf_op jit(solution)/shard_map/reduce_scatter | solution.py:286
  117.9 66.2 %reduce-scatter.14.cloned.1.call-start = ((), (), s32[]{:S(2)}) async-start(), calls=%async_computation.14 | async-start | bytes 983040 | tf_op jit(solution)/shard_map/reduce_scatter | solution.py:283
  122.1 2.0 copy-start.15
  122.1 2.0 copy-start.27
  124.0 1.9 copy-start.24
  124.0 1.9 copy-start.50
  124.0 3.0 copy-start.25
  131.2 5.2 %copy-start.6 = (bf16[256,768]{1,0:T(8,128)(2,1)S(1)}, bf16[256,768]{1,0:T(8,128)(2,1)}, u32[]{:S(2)}) copy-start(bf16[256,768]{1,0:T(8,128)(2,1)} %param.19) | copy-start | bytes 1179652
  136.4 2.6 copy-start.47
  138.9 73.9 %reduce-scatter.12.cloned.1.call-start = ((), (), s32[]{:S(2)}) async-start(), calls=%async_computation.13 | async-start | bytes 1310720 | tf_op jit(solution)/shard_map/reduce_scatter | solution.py:281
  138.9 2.2 copy-start.23
  139.0 3.3 copy-start.14
  142.2 1.8 copy-start.31
  142.2 1.8 copy-start.33
  142.2 1.8 copy-start.35
  142.3 1.8 copy-start.37
  142.3 1.8 copy-start.39
  142.3 1.8 copy-start.41
  142.3 1.8 copy-start.43
  143.9 16.0 %copy-start.48 = (f32[256]{0:T(256)S(1)}, f32[256]{0:T(256)}, u32[]{:S(2)}) copy-start(f32[256]{0:T(256)} %param.14) | copy-start | bytes 3076
  144.0 97.0 %reduce-scatter.8.cloned.1.call-start = ((), (), s32[]{:S(2)}) async-start(), calls=%async_computation.11 | async-start | bytes 1310720 | tf_op jit(solution)/shard_map/reduce_scatter | solution.py:279
  147.8 6.2 %collective-permute-start.5 = (f32[1,16,1024]{2,1,0:T(8,128)S(1)}, f32[1,16,1024]{2,1,0:T(8,128)S(1)}, u32[]{:S(2)}, u32[]{:S(2)}) collective-permute-start(f32[1,16,1024]{2,1,0:T(8,128)S(1)} %get-tuple-element.48), channel_id=1, source_target_pairs={{4,0},{5,1},{6,2},{7,3},{12,8},{13,9},{14,10},{15,11},{20,16},{21,... | collective-permute-start | bytes 196616 | tf_op jit(solution)/shard_map/ppermute | solution.py:29
  149.1 6.4 %collective-permute-start.4 = (f32[1,16,1024]{2,1,0:T(8,128)S(1)}, f32[1,16,1024]{2,1,0:T(8,128)S(1)}, u32[]{:S(2)}, u32[]{:S(2)}) collective-permute-start(f32[1,16,1024]{2,1,0:T(8,128)S(1)} %get-tuple-element.47), channel_id=1, source_target_pairs={{0,4},{1,5},{2,6},{3,7},{8,12},{9,13},{10,14},{11,15},{16,20},{17,... | collective-permute-start | bytes 196616 | tf_op jit(solution)/shard_map/ppermute | solution.py:27
  155.6 4.5 %collective-permute-start.6 = (f32[18,1,1024]{2,1,0:T(1,128)S(1)}, f32[18,1,1024]{2,1,0:T(1,128)S(1)}, u32[]{:S(2)}, u32[]{:S(2)}) collective-permute-start(f32[18,1,1024]{2,1,0:T(1,128)S(1)} %get-tuple-element.45), channel_id=1, source_target_pairs={{1,0},{2,1},{3,2},{5,4},{6,5},{7,6},{9,8},{10,9},{11,10},{13,12},{... | collective-permute-start | bytes 221192 | tf_op jit(solution)/shard_map/ppermute | solution.py:29
  156.9 3.9 %collective-permute-start.7 = (f32[18,1,1024]{2,1,0:T(1,128)S(1)}, f32[18,1,1024]{2,1,0:T(1,128)S(1)}, u32[]{:S(2)}, u32[]{:S(2)}) collective-permute-start(f32[18,1,1024]{2,1,0:T(1,128)S(1)} %get-tuple-element.46), channel_id=1, source_target_pairs={{0,1},{1,2},{2,3},{4,5},{5,6},{6,7},{8,9},{9,10},{10,11},{12,13},{... | collective-permute-start | bytes 221192 | tf_op jit(solution)/shard_map/ppermute | solution.py:27
  163.3 1.5 copy-start.53
  163.3 2.7 copy-start.10
  163.3 3.5 %copy-start.21 = (bf16[256,256]{1,0:T(8,128)(2,1)S(1)}, bf16[256,256]{1,0:T(8,128)(2,1)}, u32[]{:S(2)}) copy-start(bf16[256,256]{1,0:T(8,128)(2,1)} %param.23) | copy-start | bytes 393220
  164.6 96.8 %reduce-scatter.10.cloned.1.call-start = ((), (), s32[]{:S(2)}) async-start(), calls=%async_computation.12 | async-start | bytes 81920 | tf_op jit(solution)/shard_map/reduce_scatter | solution.py:280
  167.6 73.6 %copy-start.51 = (f32[256]{0:T(256)S(1)}, f32[256]{0:T(256)}, u32[]{:S(2)}) copy-start(f32[256]{0:T(256)} %get-tuple-element.21) | copy-start | bytes 3076
  167.6 73.6 %copy-start.52 = (f32[256]{0:T(256)S(1)}, f32[256]{0:T(256)}, u32[]{:S(2)}) copy-start(f32[256]{0:T(256)} %get-tuple-element.23) | copy-start | bytes 3076
  167.6 154.2 %all-reduce.23.cloned.1.call-start = ((), (), s32[]{:S(2)}) async-start(), calls=%async_computation.18 | async-start | bytes 2097152 | tf_op jit(solution)/shard_map/psum | solution.py:262
  321.9 8.1 %copy-start.44 = (f32[64,256]{1,0:T(8,128)S(1)}, f32[64,256]{1,0:T(8,128)}, u32[]{:S(2)}) copy-start(f32[64,256]{1,0:T(8,128)} %get-tuple-element.97) | copy-start | bytes 196612
  (8 other events, 7.8 us)
Sparse Core Ops, SparseCore 0:
  92.4 20.0 reduce-scatter.15
  115.4 20.1 reduce-scatter.19
  137.9 21.5 reduce-scatter.17
  161.6 22.3 reduce-scatter.13
  186.2 26.5 reduce-scatter.11
  215.1 25.7 reduce-scatter.7
  243.7 17.6 reduce-scatter.9
  265.7 56.1 all-reduce.22
where the time goes:
time: 339 us; the launch traced here: 337 us
  waiting for transfers between devices  124 us (37%)
  local copies, waits for them, and re-layouts  51.3 us (15%)
  blocking collectives  48.9 us (14%)
  matrix products  42.2 us (12%)
  starting transfers between devices  32 us (9%)
  other arithmetic  23 us (7%)
  between operations  16 us (5%)
    psum x1, waiting for transfers between devices, body(): lax.psum((local_grads[0], local_grads[1], local_grads[2], local_grads[3],...  35.9 us
    reduce_scatter x1, waiting for transfers between devices, body(): lax.psum_scatter(whole_sums[3], 'rep', scatter_dimension=0, tiled=True)  28.8 us
    reduce_scatter x1, waiting for transfers between devices, body(): lax.psum_scatter(whole_sums[1], 'rep', scatter_dimension=0, tiled=True)  28.1 us
    psum x1, blocking collectives, body(): lax.psum((local_grads[0], local_grads[1], local_grads[2], local_grads[3],...  23.7 us
    all_to_all x2, blocking collectives, swap_blocks(): lax.all_to_all(as_sent(flattened), ('sy', 'sx'), split_axis=0, concat_axi...  15.8 us
    reduce_scatter x1, waiting for transfers between devices, body(): lax.psum_scatter(whole_sums[5], 'rep', scatter_dimension=0, tiled=True)  15.5 us
    ppermute x4, starting transfers between devices, extended_2(): lax.ppermute(tail, axis, [(i, (i + 1) % count) for i in range(ends)])  15.5 us
    unnamed x118, local copies, waits for them, and re-layouts  11.9 us
  transfers between devices with their start and end apart: 18, of which 10 were waited for; matrix products, arithmetic and copies ran while one was open for 21% of the time, Pallas kernels for 0%

commit v1 on v0

--- a/solution.py
+++ b/solution.py
@@ -260,19 +260,22 @@
         outer_sum(grid_home, tap_grid_out),
     )
     whole_sums = lax.psum(
-        (
-            local_grads[0],
-            local_grads[1],
-            local_grads[2],
-            local_grads[3],
-            local_grads[4],
-            local_grads[5],
-            local_grads[6],
-            local_grads[7],
-            local_grads[8],
-            local_grads[9],
+        lax.psum(
+            (
+                local_grads[0],
+                local_grads[1],
+                local_grads[2],
+                local_grads[3],
+                local_grads[4],
+                local_grads[5],
+                local_grads[6],
+                local_grads[7],
+                local_grads[8],
+                local_grads[9],
+            ),
+            "sx",
         ),
-        ("sy", "sx"),
+        "sy",
     )
     summed = (
         lax.psum_scatter(whole_sums[0], "rep", scatter_dimension=0, tiled=True),

time: 339 us -> 361 us (1.065)
  waiting for transfers between devices: 124 us -> 147 us
    psum x0 -> x1, waiting for transfers between devices: none -> 21.5 us  [body(): lax.psum(lax.psum((local_grads[0], local_grads[1], local_grads[2], local_...]
    psum x1, blocking collectives: 23.7 us -> 10.6 us  [body(): lax.psum((local_grads[0], local_grads[1], local_grads[2], local_grads[3],...]
    psum x0 -> x1, blocking collectives: none -> 9.37 us  [body(): lax.psum(lax.psum((local_grads[0], local_grads[1], local_grads[2], local_...]
    reduce_scatter x1, waiting for transfers between devices: 15.5 us -> 19.5 us  [body(): lax.psum_scatter(whole_sums[5], 'rep', scatter_dimension=0, tiled=True)]
  transfers between devices with their start and end apart: 18 -> 19, of which waited for: 10 -> 11; matrix products, arithmetic and copies ran while one was open for 21% -> 20% of each run, Pallas kernels for 0% -> 0%
where the time goes in v1:
time: 361 us; the launch traced here: 359 us
  waiting for transfers between devices  147 us (41%)
  local copies, waits for them, and re-layouts  51.3 us (14%)
  blocking collectives  47.5 us (13%)
  matrix products  42.2 us (12%)
  starting transfers between devices  32.1 us (9%)
  other arithmetic  23 us (6%)
  between operations  15.7 us (4%)
    psum x1, waiting for transfers between devices, body(): lax.psum((local_grads[0], local_grads[1], local_grads[2], local_grads[3],...  34.8 us
    reduce_scatter x1, waiting for transfers between devices, body(): lax.psum_scatter(whole_sums[3], 'rep', scatter_dimension=0, tiled=True)  28.5 us
    reduce_scatter x1, waiting for transfers between devices, body(): lax.psum_scatter(whole_sums[1], 'rep', scatter_dimension=0, tiled=True)  28.1 us
    psum x1, waiting for transfers between devices, body(): lax.psum(lax.psum((local_grads[0], local_grads[1], local_grads[2], local_...  21.5 us
    reduce_scatter x1, waiting for transfers between devices, body(): lax.psum_scatter(whole_sums[5], 'rep', scatter_dimension=0, tiled=True)  19.5 us
    all_to_all x2, blocking collectives, swap_blocks(): lax.all_to_all(as_sent(flattened), ('sy', 'sx'), split_axis=0, concat_axi...  15.8 us
    ppermute x4, starting transfers between devices, extended_2(): lax.ppermute(tail, axis, [(i, (i + 1) % count) for i in range(ends)])  15.5 us
    unnamed x118, local copies, waits for them, and re-layouts  11.9 us
  transfers between devices with their start and end apart: 19, of which 11 were waited for; matrix products, arithmetic and copies ran while one was open for 20% of the time, Pallas kernels for 0%

profile of v1, /device:TPU:0, one launch (start us, length us, event | category | flops | bytes accessed | tf_op | source)
XLA Modules:
  0.0 359.2 jit_solution(12068429778434549525)
XLA Ops:
  9.5 2.4 multiply_convert_fusion.1
  11.8 1.4 collective-permute-start.1
  13.3 4.9 %collective-permute-start = (bf16[1,16,1024]{2,1,0:T(8,128)(2,1)S(1)}, bf16[1,16,1024]{2,1,0:T(8,128)(2,1)S(1)}, u32[]{:S(2)}, u32[]{:S(2)}) collective-permute-start(bf16[1,16,1024]{2,1,0:T(8,128)(2,1)S(1)} %get-tuple-element.61), channel_id=1, source_target_pairs={{0,4},{1,5},{2,6},{3,7},{8,12},{9,13},{10,14},{11,15},{16,20},{17,... | collective-permute-start | bytes 98312 | tf_op jit(solution)/shard_map/ppermute | solution.py:27
  19.2 4.0 %all-to-all-start.2 = ((bf16[8,8,4,256]{3,1,2,0:T(8,128)(2,1)}), bf16[8,8,4,256]{3,1,2,0:T(8,128)(2,1)}, u32[]{:S(2)}, u32[]{:S(2)}) async-start(bf16[8,8,4,256]{3,1,2,0:T(8,128)(2,1)} %bitcast.44), calls=%async_computation.2 | async-start | bytes 262144 | tf_op jit(solution)/shard_map/all_to_all | solution.py:135
  23.3 1.3 collective-permute-start.3
  24.6 3.0 collective-permute-start.2
  33.3 3.2 fusion.105
  36.5 1.5 fusion.6
  42.3 6.8 %all-to-all-start = ((bf16[8,8,4,256]{3,1,2,0:T(8,128)(2,1)}), bf16[8,8,4,256]{3,1,2,0:T(8,128)(2,1)}, u32[]{:S(2)}, u32[]{:S(2)}) async-start(bf16[8,8,4,256]{3,1,2,0:T(8,128)(2,1)} %bitcast.24), calls=%async_computation | async-start | bytes 262144 | tf_op jit(solution)/shard_map/all_to_all | solution.py:135
  50.8 1.2 reshape_reshape.26
  53.1 1.6 all-to-all-done
  55.8 1.3 convolution_convert_fusion.3
  57.8 1.7 copy.143
  59.6 1.7 copy.144
  62.1 2.5 fusion.107
  64.7 1.8 fusion.15
  69.8 1.8 copy.160
  71.6 1.7 copy.158
  73.3 1.7 copy.156
  77.4 7.9 %all_to_all.20 = bf16[8,8,4,256]{3,1,2,0:T(8,128)(2,1)S(1)} all-to-all(bf16[8,8,4,256]{3,1,2,0:T(8,128)(2,1)S(1)} %bitcast.291), channel_id=1, replica_groups=mesh['rep'=4,'sy'=2,'sx'=4] {'sy','sx'}, dimensions={0} | all-to-all | bytes 262144 | tf_op jit(solution)/shard_map/all_to_all | solution.py:135
  88.2 1.5 multiply_reduce_fusion.9
  89.8 1.6 fusion.96
  92.5 2.2 fusion.7
  94.8 2.1 copy.147
  96.8 2.1 reshape.413
  98.9 1.7 copy.148
  100.6 1.6 reshape_reshape.24
  103.2 7.9 %all_to_all.21 = bf16[8,8,4,256]{3,1,2,0:T(8,128)(2,1)S(1)} all-to-all(bf16[8,8,4,256]{3,1,2,0:T(8,128)(2,1)S(1)} %bitcast.293), channel_id=1, replica_groups=mesh['rep'=4,'sy'=2,'sx'=4] {'sy','sx'}, dimensions={0} | all-to-all | bytes 262144 | tf_op jit(solution)/shard_map/all_to_all | solution.py:135
  111.8 1.6 reshape_reshape.29
  113.4 1.9 fusion.112
  115.4 1.3 multiply_divide_fusion
  116.7 1.2 fusion.111
  118.0 1.2 fusion.114
  119.9 1.2 reshape.428
  122.1 1.9 fusion.20
  124.1 1.9 convolution_convert_fusion.5
  127.1 2.5 convolution_convert_fusion.6
  129.6 1.7 copy.170
  131.3 2.4 convolution_convert_fusion.7
  133.7 1.7 copy.167
  136.8 2.1 fusion.109
  142.4 1.6 convolution_bitcast_fusion
  144.2 3.7 %multiply_reduce_fusion.8 = (f32[1024]{0:T(1024)S(1)}, f32[1024]{0:T(1024)S(1)}, f32[1024]{0:T(1024)S(1)}, f32[1024]{0:T(1024)S(1)}, f32[1024]{0:T(1024)S(1)}, /...) fusion(f32[18,18,1024]{2,1,0:T(8,128)S(1)} %convert_element_typ, ...), kind=kLoop, calls=%fused_computation.104 | loop fusion | flops 14408704 | bytes 11083776 | tf_op jit(solution)/shard_map/transpose(jvp())/reduce_sum | solution.py:112
  147.8 1.3 collective-permute-start.5
  149.1 4.5 %collective-permute-start.4 = (f32[1,16,1024]{2,1,0:T(8,128)S(1)}, f32[1,16,1024]{2,1,0:T(8,128)S(1)}, u32[]{:S(2)}, u32[]{:S(2)}) collective-permute-start(f32[1,16,1024]{2,1,0:T(8,128)S(1)} %get-tuple-element.57), channel_id=1, source_target_pairs={{0,4},{1,5},{2,6},{3,7},{8,12},{9,13},{10,14},{11,15},{16,20},{17,... | collective-permute-start | bytes 196616 | tf_op jit(solution)/shard_map/ppermute | solution.py:27
  154.0 1.6 collective-permute-done.4
  155.7 1.3 collective-permute-start.6
  157.0 3.0 collective-permute-start.7
  161.4 1.9 fusion.22
  163.4 1.3 fusion.108
  164.9 19.5 %reduce-scatter.14.cloned.1.call-done = f32[64,768]{1,0:T(8,128)} async-done(((f32[256,768]{1,0:T(8,128)}), f32[64,768]{1,0:T(8,128)}) %reduce-scatter.14.cloned.1.call-update) | async-done | bytes 196624 | tf_op jit(solution)/shard_map/reduce_scatter | solution.py:286
  184.4 28.5 %reduce-scatter.12.cloned.1.call-done = f32[256,256]{1,0:T(8,128)} async-done(((f32[1024,256]{1,0:T(8,128)}), f32[256,256]{1,0:T(8,128)}) %reduce-scatter.12.cloned.1.call-update) | async-done | bytes 262160 | tf_op jit(solution)/shard_map/reduce_scatter | solution.py:284
  212.9 28.1 %reduce-scatter.8.cloned.1.call-done = f32[64,1024]{1,0:T(8,128)} async-done(((f32[256,1024]{1,0:T(8,128)}), f32[64,1024]{1,0:T(8,128)}) %reduce-scatter.8.cloned.1.call-update) | async-done | bytes 262160 | tf_op jit(solution)/shard_map/reduce_scatter | solution.py:282
  244.7 34.8 %all-reduce.26.cloned.1.call-done = (f32[64,1024]{1,0:T(8,128)}, f32[256,256]{1,0:T(8,128)}, f32[64,768]{1,0:T(8,128)}, f32[64,256]{1,0:T(8,128)}, f32[64,768]{1,0:T(8,128)}, /*index=5*/f32[64,256]{1,0:T(8,128)}) async-done(((f32[64,1024]{1,0:T(8,128)}, f32[256,256]{1,0:T(8,128)}, f32[64,768]{1,0:T(8,128)}, f32[64,256]{1,0:T(8,128)}, f32[64,768]{1,0:T(8,128)}, /*index=5*/f32[64,256]{1,0:T(8,128)}), ...) | async-done | bytes 1048592 | tf_op jit(solution)/shard_map/psum | solution.py:263
  280.0 11.7 %all-reduce.20 = (f32[256]{0:T(256)S(1)}, f32[256]{0:T(256)S(1)}, f32[256]{0:T(256)S(1)}) all-reduce(f32[256]{0:T(256)S(1)} %get-tuple-element.25, f32[256]{0:T(256)S(1)} %copy-done.52, f32[256]{0:T(256)S(1)} %copy-done.51), channel_id=2, replica_groups=mesh['rep'=4,'sy'=2,'sx'=4] {'rep'}, use_global_device_ids=true, to_apply=%region_21.0.clone | all-reduce | flops 768 | bytes 6144
  291.9 9.7 %reduce-scatter.10.cloned.1.call-done = f32[256,9]{0,1:T(8,128)} async-done(((f32[1024,9]{0,1:T(8,128)}), f32[256,9]{0,1:T(8,128)}) %reduce-scatter.10.cloned.1.call-update) | async-done | bytes 9232 | tf_op jit(solution)/shard_map/reduce_scatter | solution.py:283
  301.6 10.6 %all-reduce.18 = (f32[64]{0:T(128)S(1)}, f32[256,9]{0,1:T(8,128)S(1)}, f32[64]{0:T(128)S(1)}, f32[64]{0:T(128)S(1)}) all-reduce(f32[64]{0:T(128)S(1)} %dynamic-slice.1, f32[256,9]{0,1:T(8,128)} %reduce-scatter.10.cloned.1.call-done, f32[64]{0:T(128)S(1)} %dynamic-slice.3, ...), channel_id=1, replica_groups=mesh['rep'=4,'sy'=2,'sx'=4] {'sx'}, use_global_device_ids=true, to_apply=%region_19.0 | all-reduce | flops 2496 | bytes 19968 | tf_op jit(solution)/shard_map/psum | solution.py:263
  312.2 9.4 %all-reduce.21 = (f32[64]{0:T(128)}, f32[256,9]{0,1:T(8,128)}, f32[64]{0:T(128)}, f32[64]{0:T(128)}) all-reduce(f32[64]{0:T(128)S(1)} %get-tuple-element.27, f32[256,9]{0,1:T(8,128)S(1)} %get-tuple-element.28, f32[64]{0:T(128)S(1)} %get-tuple-element.29, f32[64]{0:T(128)S(1)} %get-tuple-element.30), channel_id=1, replica_groups=mesh['rep'=4,'sy'=2,'sx'=4] {'sy'}, use_global_device_ids=true, to_apply=%region_20.0 | all-reduce | flops 2496 | bytes 19968 | tf_op jit(solution)/shard_map/psum | solution.py:262
  322.5 21.5 %all-reduce.28.cloned.1.call-done = (f32[64,1024]{1,0:T(8,128)}, f32[256,256]{1,0:T(8,128)}, f32[64,768]{1,0:T(8,128)}, f32[64,256]{1,0:T(8,128)}, f32[64,768]{1,0:T(8,128)}, /*index=5*/f32[64,256]{1,0:T(8,128)}) async-done(((f32[64,1024]{1,0:T(8,128)}, f32[256,256]{1,0:T(8,128)}, f32[64,768]{1,0:T(8,128)}, f32[64,256]{1,0:T(8,128)}, f32[64,768]{1,0:T(8,128)}, /*index=5*/f32[64,256]{1,0:T(8,128)}), ...) | async-done | bytes 1048592 | tf_op jit(solution)/shard_map/psum | solution.py:262
  344.0 1.7 copy.205
  345.7 1.7 copy.206
  347.3 1.6 copy.207
  349.0 1.5 copy.208
  350.4 1.6 copy.209
  (235 shorter events, 44.5 us)
Async XLA Ops:
  7.2 2.3 copy-start
  8.3 9.9 %copy-start.8 = (bf16[1,16,16,256]{3,2,1,0:T(8,128)(2,1)S(1)}, bf16[1,16,16,256]{3,2,1,0:T(8,128)(2,1)}, u32[]{:S(2)}) copy-start(bf16[1,16,16,256]{3,2,1,0:T(8,128)(2,1)} %param.13) | copy-start | bytes 393220
  8.3 9.9 %copy-start.20 = (bf16[256,256]{1,0:T(8,128)(2,1)S(1)}, bf16[256,256]{1,0:T(8,128)(2,1)}, u32[]{:S(2)}) copy-start(bf16[256,256]{1,0:T(8,128)(2,1)} %param.23) | copy-start | bytes 393220
  11.8 15.9 %copy-start.45 = (f32[1024,9]{0,1:T(8,128)S(1)}, f32[1024,9]{0,1:T(8,128)}, u32[]{:S(2)}) copy-start(f32[1024,9]{0,1:T(8,128)} %param.16) | copy-start | bytes 110596
  11.8 11.4 %collective-permute-start.1 = (bf16[1,16,1024]{2,1,0:T(8,128)(2,1)S(1)}, bf16[1,16,1024]{2,1,0:T(8,128)(2,1)S(1)}, u32[]{:S(2)}, u32[]{:S(2)}) collective-permute-start(bf16[1,16,1024]{2,1,0:T(8,128)(2,1)S(1)} %get-tuple-element.62), channel_id=1, source_target_pairs={{4,0},{5,1},{6,2},{7,3},{12,8},{13,9},{14,10},{15,11},{20,16},{21,... | collective-permute-start | bytes 98312 | tf_op jit(solution)/shard_map/ppermute | solution.py:29
  13.3 9.9 %collective-permute-start = (bf16[1,16,1024]{2,1,0:T(8,128)(2,1)S(1)}, bf16[1,16,1024]{2,1,0:T(8,128)(2,1)S(1)}, u32[]{:S(2)}, u32[]{:S(2)}) collective-permute-start(bf16[1,16,1024]{2,1,0:T(8,128)(2,1)S(1)} %get-tuple-element.61), channel_id=1, source_target_pairs={{0,4},{1,5},{2,6},{3,7},{8,12},{9,13},{10,14},{11,15},{16,20},{17,... | collective-permute-start | bytes 98312 | tf_op jit(solution)/shard_map/ppermute | solution.py:27
  19.2 23.2 %all-to-all-start.2 = ((bf16[8,8,4,256]{3,1,2,0:T(8,128)(2,1)}), bf16[8,8,4,256]{3,1,2,0:T(8,128)(2,1)}, u32[]{:S(2)}, u32[]{:S(2)}) async-start(bf16[8,8,4,256]{3,1,2,0:T(8,128)(2,1)} %bitcast.44), calls=%async_computation.2 | async-start | bytes 262144 | tf_op jit(solution)/shard_map/all_to_all | solution.py:135
  23.3 4.5 %collective-permute-start.3 = (bf16[18,1,1024]{2,1,0:T(2,128)(2,1)S(1)}, bf16[18,1,1024]{2,1,0:T(2,128)(2,1)S(1)}, u32[]{:S(2)}, u32[]{:S(2)}) collective-permute-start(bf16[18,1,1024]{2,1,0:T(2,128)(2,1)S(1)} %get-tuple-element.60), channel_id=1, source_target_pairs={{1,0},{2,1},{3,2},{5,4},{6,5},{7,6},{9,8},{10,9},{11,10},{13,12},{... | collective-permute-start | bytes 110600 | tf_op jit(solution)/shard_map/ppermute | solution.py:29
  24.6 3.9 %collective-permute-start.2 = (bf16[18,1,1024]{2,1,0:T(2,128)(2,1)S(1)}, bf16[18,1,1024]{2,1,0:T(2,128)(2,1)S(1)}, u32[]{:S(2)}, u32[]{:S(2)}) collective-permute-start(bf16[18,1,1024]{2,1,0:T(2,128)(2,1)S(1)} %get-tuple-element.59), channel_id=1, source_target_pairs={{0,1},{1,2},{2,3},{4,5},{5,6},{6,7},{8,9},{9,10},{10,11},{12,13},{... | collective-permute-start | bytes 110600 | tf_op jit(solution)/shard_map/ppermute | solution.py:27
  27.7 1.5 copy-start.30
  27.7 1.5 copy-start.32
  27.7 1.5 copy-start.34
  27.8 1.5 copy-start.36
  27.8 1.5 copy-start.38
  27.8 1.5 copy-start.40
  27.8 1.5 copy-start.42
  31.6 4.8 %copy-start.7 = (bf16[2,8,2,8,256]{4,3,1,2,0:T(8,128)(2,1)}, bf16[2,8,2,8,256]{4,3,1,2,0:T(8,128)(2,1)S(1)}, u32[]{:S(2)}) copy-start(bf16[2,8,2,8,256]{4,3,1,2,0:T(8,128)(2,1)S(1)} %copy.133) | copy-start | bytes 393220
  32.3 4.2 %copy-start.18 = (bf16[4,64,256]{1,2,0:T(8,128)(2,1)}, bf16[4,64,256]{1,2,0:T(8,128)(2,1)S(1)}, u32[]{:S(2)}) copy-start(bf16[4,64,256]{1,2,0:T(8,128)(2,1)S(1)} %copy.134) | copy-start | bytes 393220
  33.3 3.2 copy-start.26
  42.3 12.4 %all-to-all-start = ((bf16[8,8,4,256]{3,1,2,0:T(8,128)(2,1)}), bf16[8,8,4,256]{3,1,2,0:T(8,128)(2,1)}, u32[]{:S(2)}, u32[]{:S(2)}) async-start(bf16[8,8,4,256]{3,1,2,0:T(8,128)(2,1)} %bitcast.24), calls=%async_computation | async-start | bytes 262144 | tf_op jit(solution)/shard_map/all_to_all | solution.py:135
  49.1 115.7 %reduce-scatter.16.cloned.1.call-start = ((), (), s32[]{:S(2)}) async-start(), calls=%async_computation.15 | async-start | bytes 327680 | tf_op jit(solution)/shard_map/reduce_scatter | solution.py:287
  57.1 7.6 %copy-start.17 = (bf16[4,64,8,32]{1,3,2,0:T(8,128)(2,1)S(1)}, bf16[4,64,8,32]{1,3,2,0:T(8,128)(2,1)}, u32[]{:S(2)}) copy-start(bf16[4,64,8,32]{1,3,2,0:T(8,128)(2,1)} %copy.154) | copy-start | bytes 393220
  64.7 4.1 %copy-start.49 = (f32[4,8,64]{2,1,0:T(8,128)}, f32[4,8,64]{2,1,0:T(8,128)S(1)}, u32[]{:S(2)}) copy-start(f32[4,8,64]{2,1,0:T(8,128)S(1)} %get-tuple-element.90) | copy-start | bytes 24580
  64.7 1.9 copy-start.16
  64.7 1.9 copy-start.29
  69.8 7.1 %copy-start.4 = (bf16[256,768]{1,0:T(8,128)(2,1)S(1)}, bf16[256,768]{1,0:T(8,128)(2,1)}, u32[]{:S(2)}) copy-start(bf16[256,768]{1,0:T(8,128)(2,1)} %param.22) | copy-start | bytes 1179652
  77.2 12.6 %copy-start.9 = (bf16[1,16,16,256]{3,2,1,0:T(8,128)(2,1)S(1)}, bf16[1,16,16,256]{3,2,1,0:T(8,128)(2,1)}, u32[]{:S(2)}) copy-start(bf16[1,16,16,256]{3,2,1,0:T(8,128)(2,1)} %param.13) | copy-start | bytes 393220
  87.3 4.1 %copy-start.12 = (bf16[2,8,2,8,256]{4,3,2,1,0:T(8,128)(2,1)S(1)}, bf16[2,8,2,8,256]{4,3,2,1,0:T(8,128)(2,1)}, u32[]{:S(2)}) copy-start(bf16[2,8,2,8,256]{4,3,2,1,0:T(8,128)(2,1)} %copy-done.11) | copy-start | bytes 393220
  92.3 72.5 %reduce-scatter.20.cloned.1.call-start = ((), (), s32[]{:S(2)}) async-start(), calls=%async_computation.17 | async-start | bytes 327680 | tf_op jit(solution)/shard_map/reduce_scatter | solution.py:290
  94.8 22.0 %copy-start.3 = (bf16[4,64,768]{2,1,0:T(8,128)(2,1)S(1)}, bf16[4,64,768]{2,1,0:T(8,128)(2,1)}, u32[]{:S(2)}) copy-start(bf16[4,64,768]{2,1,0:T(8,128)(2,1)} %copy-done.2) | copy-start | bytes 1179652
  115.4 49.5 %reduce-scatter.18.cloned.1.call-start = ((), (), s32[]{:S(2)}) async-start(), calls=%async_computation.16 | async-start | bytes 983040 | tf_op jit(solution)/shard_map/reduce_scatter | solution.py:289
  118.0 66.4 %reduce-scatter.14.cloned.1.call-start = ((), (), s32[]{:S(2)}) async-start(), calls=%async_computation.14 | async-start | bytes 983040 | tf_op jit(solution)/shard_map/reduce_scatter | solution.py:286
  122.1 2.0 copy-start.15
  122.1 2.0 copy-start.27
  124.0 1.9 copy-start.24
  124.1 1.9 copy-start.50
  124.1 3.0 copy-start.25
  131.3 5.2 %copy-start.6 = (bf16[256,768]{1,0:T(8,128)(2,1)S(1)}, bf16[256,768]{1,0:T(8,128)(2,1)}, u32[]{:S(2)}) copy-start(bf16[256,768]{1,0:T(8,128)(2,1)} %param.19) | copy-start | bytes 1179652
  136.5 2.5 copy-start.47
  138.9 73.9 %reduce-scatter.12.cloned.1.call-start = ((), (), s32[]{:S(2)}) async-start(), calls=%async_computation.13 | async-start | bytes 1310720 | tf_op jit(solution)/shard_map/reduce_scatter | solution.py:284
  139.0 2.2 copy-start.23
  139.0 3.3 copy-start.14
  142.3 1.8 copy-start.31
  142.3 1.8 copy-start.33
  142.3 1.8 copy-start.35
  142.3 1.8 copy-start.37
  142.4 1.8 copy-start.39
  142.4 1.8 copy-start.41
  142.4 1.8 copy-start.43
  144.0 16.0 %copy-start.48 = (f32[256]{0:T(256)S(1)}, f32[256]{0:T(256)}, u32[]{:S(2)}) copy-start(f32[256]{0:T(256)} %param.14) | copy-start | bytes 3076
  144.0 96.9 %reduce-scatter.8.cloned.1.call-start = ((), (), s32[]{:S(2)}) async-start(), calls=%async_computation.11 | async-start | bytes 1310720 | tf_op jit(solution)/shard_map/reduce_scatter | solution.py:282
  147.8 6.2 %collective-permute-start.5 = (f32[1,16,1024]{2,1,0:T(8,128)S(1)}, f32[1,16,1024]{2,1,0:T(8,128)S(1)}, u32[]{:S(2)}, u32[]{:S(2)}) collective-permute-start(f32[1,16,1024]{2,1,0:T(8,128)S(1)} %get-tuple-element.58), channel_id=1, source_target_pairs={{4,0},{5,1},{6,2},{7,3},{12,8},{13,9},{14,10},{15,11},{20,16},{21,... | collective-permute-start | bytes 196616 | tf_op jit(solution)/shard_map/ppermute | solution.py:29
  149.1 6.4 %collective-permute-start.4 = (f32[1,16,1024]{2,1,0:T(8,128)S(1)}, f32[1,16,1024]{2,1,0:T(8,128)S(1)}, u32[]{:S(2)}, u32[]{:S(2)}) collective-permute-start(f32[1,16,1024]{2,1,0:T(8,128)S(1)} %get-tuple-element.57), channel_id=1, source_target_pairs={{0,4},{1,5},{2,6},{3,7},{8,12},{9,13},{10,14},{11,15},{16,20},{17,... | collective-permute-start | bytes 196616 | tf_op jit(solution)/shard_map/ppermute | solution.py:27
  155.7 4.5 %collective-permute-start.6 = (f32[18,1,1024]{2,1,0:T(1,128)S(1)}, f32[18,1,1024]{2,1,0:T(1,128)S(1)}, u32[]{:S(2)}, u32[]{:S(2)}) collective-permute-start(f32[18,1,1024]{2,1,0:T(1,128)S(1)} %get-tuple-element.55), channel_id=1, source_target_pairs={{1,0},{2,1},{3,2},{5,4},{6,5},{7,6},{9,8},{10,9},{11,10},{13,12},{... | collective-permute-start | bytes 221192 | tf_op jit(solution)/shard_map/ppermute | solution.py:29
  157.0 3.9 %collective-permute-start.7 = (f32[18,1,1024]{2,1,0:T(1,128)S(1)}, f32[18,1,1024]{2,1,0:T(1,128)S(1)}, u32[]{:S(2)}, u32[]{:S(2)}) collective-permute-start(f32[18,1,1024]{2,1,0:T(1,128)S(1)} %get-tuple-element.56), channel_id=1, source_target_pairs={{0,1},{1,2},{2,3},{4,5},{5,6},{6,7},{8,9},{9,10},{10,11},{12,13},{... | collective-permute-start | bytes 221192 | tf_op jit(solution)/shard_map/ppermute | solution.py:27
  163.4 77.7 %copy-start.53 = (u32[32]{0:T(128)S(1)}, u32[32]{0:T(128)}, u32[]{:S(2)}) copy-start(u32[32]{0:T(128)} %constant.75) | copy-start | bytes 388
  163.4 79.0 %copy-start.10 = (bf16[8,2,4,4,256]{4,3,2,1,0:T(4,128)(2,1)S(1)}, bf16[8,2,4,4,256]{4,3,2,1,0:T(4,128)(2,1)}, u32[]{:S(2)}) copy-start(bf16[8,2,4,4,256]{4,3,2,1,0:T(4,128)(2,1)} %copy.150) | copy-start | bytes 393220
  163.4 79.7 %copy-start.21 = (bf16[256,256]{1,0:T(8,128)(2,1)S(1)}, bf16[256,256]{1,0:T(8,128)(2,1)}, u32[]{:S(2)}) copy-start(bf16[256,256]{1,0:T(8,128)(2,1)} %param.23) | copy-start | bytes 393220
  164.7 114.8 %all-reduce.26.cloned.1.call-start = ((), (), s32[]{:S(2)}) async-start(), calls=%async_computation.18 | async-start | bytes 2097152 | tf_op jit(solution)/shard_map/psum | solution.py:263
  241.0 60.6 %reduce-scatter.10.cloned.1.call-start = ((), (), s32[]{:S(2)}) async-start(), calls=%async_computation.12 | async-start | bytes 81920 | tf_op jit(solution)/shard_map/reduce_scatter | solution.py:283
  244.0 100.0 %all-reduce.28.cloned.1.call-start = ((), (), s32[]{:S(2)}) async-start(), calls=%async_computation.19 | async-start | bytes 2097152 | tf_op jit(solution)/shard_map/psum | solution.py:262
  244.0 36.0 %copy-start.51 = (f32[256]{0:T(256)S(1)}, f32[256]{0:T(256)}, u32[]{:S(2)}) copy-start(f32[256]{0:T(256)} %get-tuple-element.21) | copy-start | bytes 3076
  244.0 36.0 %copy-start.52 = (f32[256]{0:T(256)S(1)}, f32[256]{0:T(256)}, u32[]{:S(2)}) copy-start(f32[256]{0:T(256)} %get-tuple-element.23) | copy-start | bytes 3076
  344.0 8.1 %copy-start.44 = (f32[64,256]{1,0:T(8,128)S(1)}, f32[64,256]{1,0:T(8,128)}, u32[]{:S(2)}) copy-start(f32[64,256]{1,0:T(8,128)} %get-tuple-element.107) | copy-start | bytes 196612
  (9 other events, 9.1 us)
Sparse Core Ops, SparseCore 0:
  92.4 20.1 reduce-scatter.15
  115.5 20.1 reduce-scatter.19
  138.0 21.5 reduce-scatter.17
  161.8 22.5 reduce-scatter.13
  186.5 26.3 reduce-scatter.11
  215.1 25.7 reduce-scatter.7
  243.7 35.7 all-reduce.25
  282.4 19.1 reduce-scatter.9
  304.2 39.7 all-reduce.27
